TPU v7x, 256 devices: a whole 4x4x8 slice. The times are simulated.
256 devices in a mesh: dp: 16 (over z, core), group: 16 (over x, y).
Axes of the slice: x: 4, y: 4, z: 8, core: 2. Of those that a mesh axis runs over, the one named last changes fastest.
Arguments:
- hidden_in: bfloat16 [16, 16, 128, 5120], P('dp', 'group'), may hold values from -48 to 48
- gain: float32 [5120], replicated, may hold values from 0.1 to 1.9
- value_weight: bfloat16 [5120, 512], P(('dp', 'group')), may hold values from -0.078125 to 0.078125
- value_cot: bfloat16 [16, 16, 128, 512], P('dp', 'group'), may hold values from -6 to 6
- lengths: int32 [16, 16], P('dp', 'group'), may hold values from 1 to 128, as said below
- rewards: int32 [16, 16], P('dp', 'group'), may hold values from 0 to 3
Outputs:
- values: bfloat16 [16, 16, 128, 512], P('dp', 'group')
- weight_grad: float32 [5120, 512], P(('dp', 'group'))
- gain_grad: float32 [5120], P(('dp', 'group'))
Inputs may be any that keep to these rules, and one draw needn't show every extreme that they name: `lengths`: some response has exactly 128 tokens.
All inputs are finite; a program needn't handle non-finite values.
Results may differ from a plain program's by a relative error of at most 0.019.
Values may be sent and summed in bfloat16 or wider, within the bound.
No kernel may reach another device: no remote copies, remote signals or barrier semaphores. Data moves between devices by JAX's collectives and lax.ppermute only.
A program may use at most 64 MiB of HBM per device.

v0:
```python
import jax
import jax.numpy as jnp
from jax import lax
from jax.sharding import PartitionSpec as P


def body(hidden_in, gain, value_weight, value_cot, lengths, rewards):
    prompts, answers, length, features = hidden_in.shape
    kv_width = value_weight.shape[1]
    row_count = prompts * answers * length
    n_dp = lax.axis_size("dp")
    n_group = lax.axis_size("group")
    group_count = answers * n_group
    shard_rows = value_weight.shape[0]
    scores = rewards.astype(jnp.float32)
    peer_scores = lax.all_to_all(
        jnp.broadcast_to(scores.reshape(1, -1), (n_group, scores.size)), "group", 0, 0, tiled=True
    )
    reward_sum = jnp.sum(peer_scores).reshape(1, 1)
    square_sum = jnp.sum(peer_scores * peer_scores).reshape(1, 1)
    centre = reward_sum / group_count
    spread = square_sum / group_count - centre * centre
    advantage = (scores - centre) / jnp.maximum(jnp.sqrt(spread), 1.0)
    position = jnp.arange(length)
    alive_mask = position[None, None, :] < lengths[:, :, None]
    token_weight = jnp.where(alive_mask, (advantage / lengths.astype(jnp.float32))[:, :, None], 0.0)
    flat_in = hidden_in.reshape(row_count, features)
    inverse = lax.rsqrt(
        jnp.mean(jnp.square(flat_in.astype(jnp.float32)), axis=1, keepdims=True) + 1e-06
    )
    normed = (flat_in.astype(jnp.float32) * inverse * gain).astype(jnp.bfloat16)
    scaled_cot = (
        token_weight.reshape(row_count, 1)
        * value_cot.reshape(row_count, kv_width).astype(jnp.float32)
    ).astype(jnp.bfloat16)
    part = lax.all_to_all(
        jnp.broadcast_to(value_weight[None], (n_group,) + value_weight.shape),
        "group",
        0,
        0,
        tiled=True,
    ).reshape(n_group * shard_rows, kv_width)
    full_weight = lax.all_gather(part, "dp", axis=0, tiled=True)
    projected = jnp.dot(normed, full_weight, preferred_element_type=jnp.float32)
    back = lax.dot_general(
        scaled_cot, full_weight, (((1,), (1,)), ((), ())), preferred_element_type=jnp.float32
    )
    gain_term = jnp.sum(back * (flat_in.astype(jnp.float32) * inverse), axis=0)
    values = projected.astype(jnp.bfloat16).reshape(prompts, answers, length, kv_width)
    grad_part = lax.dot_general(
        normed, scaled_cot, (((0,), (0,)), ((), ())), preferred_element_type=jnp.float32
    )
    grad_part = lax.psum_scatter(
        grad_part.reshape(n_dp, features // n_dp, kv_width).astype(jnp.bfloat16),
        "dp",
        scatter_dimension=0,
        tiled=True,
    )
    grad_part = grad_part.astype(jnp.float32).reshape(n_group, shard_rows, kv_width)
    weight_grad = lax.all_to_all(grad_part, "group", 0, 0, tiled=True).sum(0)
    gain_part = lax.all_to_all(gain_term.reshape(n_dp, features // n_dp), "dp", 0, 0, tiled=True)
    gain_part = gain_part.sum(0).reshape(n_group, shard_rows)
    gain_grad = lax.all_to_all(gain_part, "group", 0, 0, tiled=True).sum(0)
    return (values, weight_grad, gain_grad)


def solution(mesh):
    in_specs = (
        P("dp", "group", None, None),
        P(),
        P(("dp", "group"), None),
        P("dp", "group", None, None),
        P("dp", "group"),
        P("dp", "group"),
    )
    out_specs = (P("dp", "group", None, None), P(("dp", "group"), None), P(("dp", "group")))
    return jax.shard_map(body, mesh=mesh, in_specs=in_specs, out_specs=out_specs, check_vma=False)
```

profile of v0, /device:TPU:8, one launch (start us, length us, event | category | flops | bytes accessed | tf_op | source)
XLA Modules:
  0.0 162.0 jit_solution(6888291572416146831)
XLA Ops:
  7.2 0.0 copy-start
  7.2 0.0 copy-start.2
  7.2 0.0 all-gather.2.cloned.1.call-start
  7.2 0.9 broadcast_in_dim.32
  8.1 15.4 %all_to_all.34 = bf16[16,20,512]{2,1,0:T(8,128)(2,1)S(1)} all-to-all(bf16[16,20,512]{2,1,0:T(8,128)(2,1)S(1)} %broadcast_in_dim.32), channel_id=1, replica_groups=mesh['dp'=16,'group'=16] {'group'}, dimensions={0} | all-to-all | bytes 655360 | tf_op jit(solution)/shard_map/all_to_all | solution.py:36
  23.5 0.8 reshape.96
  24.3 0.0 all-gather.2.cloned.1.call-update
  24.9 0.6 broadcast_in_dim.34
  25.5 5.3 %all-to-all-start.1 = ((f32[16,1,1]{2,1,0:T(1,128)}), f32[16,1,1]{2,1,0:T(1,128)S(1)}, u32[]{:S(2)}, u32[]{:S(2)}) async-start(f32[16,1,1]{2,1,0:T(1,128)} %broadcast_in_dim.34), calls=%async_computation.1 | async-start | bytes 16384 | tf_op jit(solution)/shard_map/all_to_all | solution.py:16
  30.9 0.0 reduce-scatter.2.cloned.1.call-start
  31.6 0.0 copy-done
  31.6 0.3 fusion.2
  31.9 5.1 %all-to-all-done.1 = f32[16,1,1]{2,1,0:T(1,128)S(1)} async-done(((f32[16,1,1]{2,1,0:T(1,128)}), f32[16,1,1]{2,1,0:T(1,128)S(1)}, u32[]{:S(2)}, u32[]{:S(2)}) %all-to-all-start.1) | async-done | bytes 96 | tf_op jit(solution)/shard_map/all_to_all | solution.py:16
  37.0 0.6 reduce_sum.64
  39.6 0.1 copy.18
  39.7 0.6 multiply_reduce_fusion
  41.0 0.0 copy-done.2
  41.1 0.0 copy-start.1
  41.1 0.4 fusion.5
  41.5 1.4 copy.17
  42.9 0.0 copy-done.1
  42.9 5.3 %convolution_convert_fusion = bf16[16,320,512]{2,1,0:T(8,128)(2,1)} fusion(bf16[16,320,128]{2,1,0:T(8,128)(2,1)} %bitcast.35, bf16[1,1,128,512]{3,2,1,0:T(8,128)(2,1)S(1)} %copy-done.1, f32[128]{0:T(128)S(1)} %get-tuple-element.3), kind=kOutput, calls=%fused_computation.4 | convolution fusion | flops 673906688 | bytes 6685184 | tf_op jit(solution)/shard_map/dot_general | solution.py:50
  48.2 0.0 reduce-scatter.2.cloned.1.call-update
  48.2 20.3 %all-gather.2.cloned.1.call-done = bf16[5120,512]{1,0:T(8,128)(2,1)} async-done(((bf16[320,512]{1,0:T(8,128)(2,1)}), bf16[5120,512]{1,0:T(8,128)(2,1)}) %all-gather.2.cloned.1.call-update) | async-done | bytes 5242896 | tf_op jit(solution)/shard_map/all_gather | solution.py:43
  68.5 4.3 %fusion.3 = f32[5120]{0:T(1024)S(1)} fusion(bf16[5120,512]{1,0:T(8,128)(2,1)} %all-gather.2.cloned.1.call-done, bf16[1,1,128,5120]{3,2,1,0:T(8,128)(2,1)S(1)} %copy-done, f32[128]{0:T(128)S(1)} %get-tuple-element.4, bf16[1,1,128,512]{3,2,1,0:T(8,128)(2,1)S(1)} %copy-done.1, f32[128]{0:T(128)S(1)} %get-tuple-element.3), kind=kOutput, calls=%fused_computation.7 | convolution fusion | flops 673901568 | bytes 6706176 | tf_op jit(solution)/shard_map/dot_general | solution.py:45
  72.8 0.1 all_to_all.25
  72.9 11.9 %all_to_all.35 = f32[16,1,320]{2,1,0:T(1,128)S(1)} all-to-all(f32[16,1,320]{2,1,0:T(1,128)S(1)} %all_to_all.25), channel_id=1, replica_groups=mesh['dp'=16,'group'=16] {'dp'}, dimensions={0} | all-to-all | bytes 40960 | tf_op jit(solution)/shard_map/all_to_all | solution.py:61
  84.8 0.7 all_to_all.27
  85.5 7.4 %all-to-all-start.4 = ((f32[16,1,20]{2,1,0:T(1,128)}), f32[16,1,20]{2,1,0:T(1,128)S(1)}, u32[]{:S(2)}, u32[]{:S(2)}) async-start(f32[16,1,20]{2,1,0:T(1,128)} %all_to_all.27), calls=%async_computation.5 | async-start | bytes 16384 | tf_op jit(solution)/shard_map/all_to_all | solution.py:63
  92.9 42.3 %reduce-scatter.2.cloned.1.call-done = bf16[1,320,512]{2,1,0:T(8,128)(2,1)} async-done(((bf16[16,320,512]{2,1,0:T(8,128)(2,1)}), bf16[1,320,512]{2,1,0:T(8,128)(2,1)}) %reduce-scatter.2.cloned.1.call-update) | async-done | bytes 327696 | tf_op jit(solution)/shard_map/reduce_scatter | solution.py:53
  135.2 1.9 %reshape.104 = f32[16,20,512]{2,1,0:T(8,128)} reshape(bf16[1,320,512]{2,1,0:T(8,128)(2,1)} %reduce-scatter.2.cloned.1.call-done) | data formatting | bytes 983040 | tf_op jit(solution)/shard_map/reshape | solution.py:59
  137.2 0.0 all-to-all-done.4
  137.2 7.1 %all-to-all-start.2 = ((f32[16,20,512]{2,1,0:T(8,128)}), f32[16,20,512]{2,1,0:T(8,128)S(1)}, u32[]{:S(2)}, u32[]{:S(2)}) async-start(f32[16,20,512]{2,1,0:T(8,128)} %reshape.104), calls=%async_computation.3 | async-start | bytes 1572864 | tf_op jit(solution)/shard_map/all_to_all | solution.py:60
  144.3 4.0 %fusion.4 = bf16[1,1,128,512]{3,2,1,0:T(8,128)(2,1)} fusion(bf16[5120,512]{1,0:T(8,128)(2,1)} %all-gather.2.cloned.1.call-done, bf16[1,1,128,5120]{3,2,1,0:T(8,128)(2,1)S(1)} %copy-done, f32[5120]{0:T(1024)S(1)} %copy-done.2, f32[128]{0:T(128)S(1)} %get-tuple-element.4), kind=kOutput, calls=%fused_computation.9 | convolution fusion | flops 673775616 | bytes 6705664 | tf_op jit(solution)/shard_map/dot_general | solution.py:44
  148.3 0.5 reduce_sum.69
  148.9 5.6 %all-to-all-done.2 = f32[16,20,512]{2,1,0:T(8,128)S(1)} async-done(((f32[16,20,512]{2,1,0:T(8,128)}), f32[16,20,512]{2,1,0:T(8,128)S(1)}, u32[]{:S(2)}, u32[]{:S(2)}) %all-to-all-start.2) | async-done | bytes 655392 | tf_op jit(solution)/shard_map/all_to_all | solution.py:60
  154.4 0.7 reduce_sum.66
  (2 shorter events, 0.0 us)
Async XLA Ops:
  7.2 24.4 %copy-start = (bf16[1,1,128,5120]{3,2,1,0:T(8,128)(2,1)S(1)}, bf16[1,1,128,5120]{3,2,1,0:T(8,128)(2,1)}, u32[]{:S(2)}) copy-start(bf16[1,1,128,5120]{3,2,1,0:T(8,128)(2,1)} %param.6) | copy-start | bytes 3932164
  7.2 33.9 %copy-start.2 = (f32[5120]{0:T(1024)S(1)}, f32[5120]{0:T(1024)}, u32[]{:S(2)}) copy-start(f32[5120]{0:T(1024)} %param.7) | copy-start | bytes 61444
  7.2 61.3 %all-gather.2.cloned.1.call-start = ((), (), s32[]{:S(2)}) async-start(), calls=%async_computation.6 | async-start | bytes 5570560 | tf_op jit(solution)/shard_map/all_gather | solution.py:43
  25.5 11.5 %all-to-all-start.1 = ((f32[16,1,1]{2,1,0:T(1,128)}), f32[16,1,1]{2,1,0:T(1,128)S(1)}, u32[]{:S(2)}, u32[]{:S(2)}) async-start(f32[16,1,1]{2,1,0:T(1,128)} %broadcast_in_dim.34), calls=%async_computation.1 | async-start | bytes 16384 | tf_op jit(solution)/shard_map/all_to_all | solution.py:16
  30.9 104.4 %reduce-scatter.2.cloned.1.call-start = ((), (), s32[]{:S(2)}) async-start(), calls=%async_computation.7 | async-start | bytes 5570560 | tf_op jit(solution)/shard_map/reduce_scatter | solution.py:53
  41.1 1.8 %copy-start.1 = (bf16[1,1,128,512]{3,2,1,0:T(8,128)(2,1)S(1)}, bf16[1,1,128,512]{3,2,1,0:T(8,128)(2,1)}, u32[]{:S(2)}) copy-start(bf16[1,1,128,512]{3,2,1,0:T(8,128)(2,1)} %param.9) | copy-start | bytes 393220
  85.5 51.7 %all-to-all-start.4 = ((f32[16,1,20]{2,1,0:T(1,128)}), f32[16,1,20]{2,1,0:T(1,128)S(1)}, u32[]{:S(2)}, u32[]{:S(2)}) async-start(f32[16,1,20]{2,1,0:T(1,128)} %all_to_all.27), calls=%async_computation.5 | async-start | bytes 16384 | tf_op jit(solution)/shard_map/all_to_all | solution.py:63
  137.2 17.3 %all-to-all-start.2 = ((f32[16,20,512]{2,1,0:T(8,128)}), f32[16,20,512]{2,1,0:T(8,128)S(1)}, u32[]{:S(2)}, u32[]{:S(2)}) async-start(f32[16,20,512]{2,1,0:T(8,128)} %reshape.104), calls=%async_computation.3 | async-start | bytes 1572864 | tf_op jit(solution)/shard_map/all_to_all | solution.py:60
Sparse Core Ops, SparseCore 0:
  24.4 44.0 all-gather.1
  71.1 64.1 reduce-scatter.1
where the time goes:
time: 163 us; the launch traced here: 162 us
  waiting for transfers between devices  73.3 us (45%)
  blocking collectives  27.2 us (17%)
  starting transfers between devices  19.9 us (12%)
  between operations  18.1 us (11%)
  matrix products  13.6 us (8%)
  local copies, waits for them, and re-layouts  6.51 us (4%)
  other arithmetic  3.2 us (2%)
    reduce_scatter x1, waiting for transfers between devices, body(): lax.psum_scatter(grad_part.reshape(n_dp, features // n_dp, kv_width).asty...  42.3 us
    all_gather x1, waiting for transfers between devices, body(): full_weight = lax.all_gather(part, 'dp', axis=0, tiled=True)  20.3 us
    all_to_all x1, blocking collectives, body(): lax.all_to_all(jnp.broadcast_to(value_weight[None], (n_group,) + value_we...  15.4 us
    all_to_all x1, blocking collectives, body(): lax.all_to_all(gain_term.reshape(n_dp, features // n_dp), 'dp', 0, 0, til...  11.9 us
    all_to_all x1, starting transfers between devices, body(): gain_grad = lax.all_to_all(gain_part, 'group', 0, 0, tiled=True).sum(0)  7.4 us
    all_to_all x1, starting transfers between devices, body(): weight_grad = lax.all_to_all(grad_part, 'group', 0, 0, tiled=True).sum(0)  7.12 us
    all_to_all x1, waiting for transfers between devices, body(): weight_grad = lax.all_to_all(grad_part, 'group', 0, 0, tiled=True).sum(0)  5.57 us
    all_to_all x1, starting transfers between devices, body(): lax.all_to_all(jnp.broadcast_to(scores.reshape(1, -1), (n_group, scores.s...  5.35 us
  transfers between devices with their start and end apart: 5, of which 4 were waited for; matrix products, arithmetic and copies ran while one was open for 12% of the time, Pallas kernels for 0%

commit v1 on v0

--- a/solution.py
+++ b/solution.py
@@ -40,7 +40,9 @@
         0,
         tiled=True,
     ).reshape(n_group * shard_rows, kv_width)
-    full_weight = lax.all_gather(part, "dp", axis=0, tiled=True)
+    full_weight = jnp.concatenate(
+        lax.all_to_all(jnp.stack([part] * lax.axis_size("dp")), "dp", 0, 0), axis=0
+    )
     projected = jnp.dot(normed, full_weight, preferred_element_type=jnp.float32)
     back = lax.dot_general(
         scaled_cot, full_weight, (((1,), (1,)), ((), ())), preferred_element_type=jnp.float32

time: 163 us -> 247 us (1.52)
  blocking collectives: 27.2 us -> 162 us
  waiting for transfers between devices: 73.3 us -> 15.7 us
  starting transfers between devices: 19.9 us -> 24.4 us
  local copies, waits for them, and re-layouts: 6.51 us -> 9.29 us
  matrix products: 13.6 us -> 11.1 us
    all_to_all x1, blocking collectives: 15.4 us -> 150 us  [body(): lax.all_to_all(jnp.stack([part] * lax.axis_size('dp')), 'dp', 0, 0)]
    reduce_scatter x1, waiting for transfers between devices: 42.3 us -> 0.01 us  [body(): lax.psum_scatter(grad_part.reshape(n_dp, features // n_dp, kv_width).asty...]
    all_gather x1 -> x0, waiting for transfers between devices: 20.3 us -> none  [body(): full_weight = lax.all_gather(part, 'dp', axis=0, tiled=True)]
    all_to_all x0 -> x1, starting transfers between devices: none -> 4.8 us  [body(): lax.all_to_all(jnp.broadcast_to(value_weight[None], (n_group,) + value_we...]
    all_to_all x1, waiting for transfers between devices: 0.01 us -> 4.22 us  [body(): gain_grad = lax.all_to_all(gain_part, 'group', 0, 0, tiled=True).sum(0)]
  transfers between devices with their start and end apart: 5 -> 5, of which waited for: 4 -> 3; matrix products, arithmetic and copies ran while one was open for 12% -> 8% of each run, Pallas kernels for 0% -> 0%
where the time goes in v1:
time: 247 us; the launch traced here: 246 us
  blocking collectives  162 us (66%)
  starting transfers between devices  24.4 us (10%)
  between operations  18.2 us (7%)
  waiting for transfers between devices  15.7 us (6%)
  matrix products  11.1 us (4%)
  local copies, waits for them, and re-layouts  9.29 us (4%)
  other arithmetic  5.28 us (2%)
    all_to_all x1, blocking collectives, body(): lax.all_to_all(jnp.stack([part] * lax.axis_size('dp')), 'dp', 0, 0)  150 us
    all_to_all x1, blocking collectives, body(): lax.all_to_all(gain_term.reshape(n_dp, features // n_dp), 'dp', 0, 0, til...  12.3 us
    all_to_all x1, waiting for transfers between devices, body(): weight_grad = lax.all_to_all(grad_part, 'group', 0, 0, tiled=True).sum(0)  7.57 us
    all_to_all x1, starting transfers between devices, body(): lax.all_to_all(jnp.broadcast_to(scores.reshape(1, -1), (n_group, scores.s...  7.39 us
    all_to_all x1, starting transfers between devices, body(): gain_grad = lax.all_to_all(gain_part, 'group', 0, 0, tiled=True).sum(0)  7.28 us
    dot_general x1, matrix products, body(): lax.dot_general(normed, scaled_cot, (((0,), (0,)), ((), ())), preferred_e...  5.21 us
  transfers between devices with their start and end apart: 5, of which 3 were waited for; matrix products, arithmetic and copies ran while one was open for 8% of the time, Pallas kernels for 0%

profile of v1, /device:TPU:8, one launch (start us, length us, event | category | flops | bytes accessed | tf_op | source)
XLA Modules:
  0.0 246.3 jit_solution(10689861893098363771)
XLA Ops:
  7.2 0.0 copy-start.1
  7.9 0.6 broadcast_in_dim.34
  8.5 7.4 %all-to-all-start.2 = ((f32[16,1,1]{2,1,0:T(1,128)}), f32[16,1,1]{2,1,0:T(1,128)S(1)}, u32[]{:S(2)}, u32[]{:S(2)}) async-start(f32[16,1,1]{2,1,0:T(1,128)} %broadcast_in_dim.34), calls=%async_computation.2 | async-start | bytes 16384 | tf_op jit(solution)/shard_map/all_to_all | solution.py:16
  16.6 1.7 fusion.4
  18.2 3.8 %all-to-all-done.2 = f32[16,1,1]{2,1,0:T(1,128)S(1)} async-done(((f32[16,1,1]{2,1,0:T(1,128)}), f32[16,1,1]{2,1,0:T(1,128)S(1)}, u32[]{:S(2)}, u32[]{:S(2)}) %all-to-all-start.2) | async-done | bytes 96 | tf_op jit(solution)/shard_map/all_to_all | solution.py:16
  22.1 1.5 broadcast_in_dim.32
  23.6 4.8 %all-to-all-start = ((bf16[16,20,512]{2,1,0:T(8,128)(2,1)}), bf16[16,20,512]{2,1,0:T(8,128)(2,1)S(1)}, u32[]{:S(2)}, u32[]{:S(2)}) async-start(bf16[16,20,512]{2,1,0:T(8,128)(2,1)} %broadcast_in_dim.32), calls=%async_computation | async-start | bytes 786432 | tf_op jit(solution)/shard_map/all_to_all | solution.py:36
  28.4 0.0 reduce-scatter.2.cloned.1.call-start
  28.4 0.6 reduce_sum.64
  31.0 0.1 copy.18
  31.1 0.6 multiply_reduce_fusion
  32.5 0.0 copy-done.1
  32.5 0.0 copy-start.2
  32.5 1.1 fusion.11
  33.6 1.5 copy.17
  35.1 0.0 copy-done.2
  35.1 5.2 %convolution_convert_fusion = bf16[16,320,512]{2,1,0:T(8,128)(2,1)} fusion(bf16[16,320,128]{2,1,0:T(8,128)(2,1)} %bitcast.50, bf16[1,1,128,512]{3,2,1,0:T(8,128)(2,1)S(1)} %copy-done.2, f32[128]{0:T(128)S(1)} %get-tuple-element.3), kind=kOutput, calls=%fused_computation.6 | convolution fusion | flops 673906688 | bytes 6685184 | tf_op jit(solution)/shard_map/dot_general | solution.py:52
  40.3 0.0 reduce-scatter.2.cloned.1.call-update
  40.3 0.0 all-to-all-done
  40.3 0.1 stack_reshape.2
  40.4 0.5 stack.3
  40.9 150.0 %all_to_all.39 = bf16[16,320,512]{2,1,0:T(8,128)(2,1)S(1)} all-to-all(bf16[16,320,512]{2,1,0:T(8,128)(2,1)S(1)} %stack.3), channel_id=1, replica_groups=mesh['dp'=16,'group'=16] {'dp'}, dimensions={0} | all-to-all | bytes 10485760 | tf_op jit(solution)/shard_map/all_to_all | solution.py:44
  191.0 0.0 copy-start
  191.0 2.3 copy-done
  193.3 1.9 fusion.7
  195.2 0.0 copy-start.3
  195.2 0.1 all_to_all.29
  195.3 12.3 %all_to_all.40 = f32[16,1,320]{2,1,0:T(1,128)S(1)} all-to-all(f32[16,1,320]{2,1,0:T(1,128)S(1)} %all_to_all.29), channel_id=1, replica_groups=mesh['dp'=16,'group'=16] {'dp'}, dimensions={0} | all-to-all | bytes 40960 | tf_op jit(solution)/shard_map/all_to_all | solution.py:63
  207.6 0.7 all_to_all.31
  208.3 7.3 %all-to-all-start.5 = ((f32[16,1,20]{2,1,0:T(1,128)}), f32[16,1,20]{2,1,0:T(1,128)S(1)}, u32[]{:S(2)}, u32[]{:S(2)}) async-start(f32[16,1,20]{2,1,0:T(1,128)} %all_to_all.31), calls=%async_computation.6 | async-start | bytes 16384 | tf_op jit(solution)/shard_map/all_to_all | solution.py:65
  215.6 0.0 reduce-scatter.2.cloned.1.call-done
  215.6 1.9 reshape.126
  217.5 4.2 %all-to-all-done.5 = f32[16,1,20]{2,1,0:T(1,128)S(1)} async-done(((f32[16,1,20]{2,1,0:T(1,128)}), f32[16,1,20]{2,1,0:T(1,128)S(1)}, u32[]{:S(2)}, u32[]{:S(2)}) %all-to-all-start.5) | async-done | bytes 1312 | tf_op jit(solution)/shard_map/all_to_all | solution.py:65
  221.8 4.9 %all-to-all-start.3 = ((f32[16,20,512]{2,1,0:T(8,128)}), f32[16,20,512]{2,1,0:T(8,128)S(1)}, u32[]{:S(2)}, u32[]{:S(2)}) async-start(f32[16,20,512]{2,1,0:T(8,128)} %reshape.126), calls=%async_computation.4 | async-start | bytes 1572864 | tf_op jit(solution)/shard_map/all_to_all | solution.py:62
  226.6 0.0 copy-done.3
  226.6 4.0 %fusion.17 = bf16[1,1,128,512]{3,2,1,0:T(8,128)(2,1)} fusion(bf16[5120,512]{1,0:T(8,128)(2,1)} %bitcast.49, bf16[1,1,128,5120]{3,2,1,0:T(8,128)(2,1)S(1)} %copy-done.1, f32[5120]{0:T(1024)S(1)} %copy-done.3, f32[128]{0:T(128)S(1)} %get-tuple-element.4), kind=kOutput, calls=%fused_computation.18 | convolution fusion | flops 673775616 | bytes 6705664 | tf_op jit(solution)/shard_map/dot_general | solution.py:46
  230.7 0.5 reduce_sum.69
  231.2 7.6 %all-to-all-done.3 = f32[16,20,512]{2,1,0:T(8,128)S(1)} async-done(((f32[16,20,512]{2,1,0:T(8,128)}), f32[16,20,512]{2,1,0:T(8,128)S(1)}, u32[]{:S(2)}, u32[]{:S(2)}) %all-to-all-start.3) | async-done | bytes 655392 | tf_op jit(solution)/shard_map/all_to_all | solution.py:62
  238.8 0.7 reduce_sum.66
  (2 shorter events, 0.0 us)
Async XLA Ops:
  7.2 25.3 %copy-start.1 = (bf16[1,1,128,5120]{3,2,1,0:T(8,128)(2,1)S(1)}, bf16[1,1,128,5120]{3,2,1,0:T(8,128)(2,1)}, u32[]{:S(2)}) copy-start(bf16[1,1,128,5120]{3,2,1,0:T(8,128)(2,1)} %param.6) | copy-start | bytes 3932164
  8.5 13.5 %all-to-all-start.2 = ((f32[16,1,1]{2,1,0:T(1,128)}), f32[16,1,1]{2,1,0:T(1,128)S(1)}, u32[]{:S(2)}, u32[]{:S(2)}) async-start(f32[16,1,1]{2,1,0:T(1,128)} %broadcast_in_dim.34), calls=%async_computation.2 | async-start | bytes 16384 | tf_op jit(solution)/shard_map/all_to_all | solution.py:16
  23.6 16.7 %all-to-all-start = ((bf16[16,20,512]{2,1,0:T(8,128)(2,1)}), bf16[16,20,512]{2,1,0:T(8,128)(2,1)S(1)}, u32[]{:S(2)}, u32[]{:S(2)}) async-start(bf16[16,20,512]{2,1,0:T(8,128)(2,1)} %broadcast_in_dim.32), calls=%async_computation | async-start | bytes 786432 | tf_op jit(solution)/shard_map/all_to_all | solution.py:36
  28.4 187.2 %reduce-scatter.2.cloned.1.call-start = ((), (), s32[]{:S(2)}) async-start(), calls=%async_computation.7 | async-start | bytes 5570560 | tf_op jit(solution)/shard_map/reduce_scatter | solution.py:55
  32.5 2.6 %copy-start.2 = (bf16[1,1,128,512]{3,2,1,0:T(8,128)(2,1)S(1)}, bf16[1,1,128,512]{3,2,1,0:T(8,128)(2,1)}, u32[]{:S(2)}) copy-start(bf16[1,1,128,512]{3,2,1,0:T(8,128)(2,1)} %param.9) | copy-start | bytes 393220
  191.0 2.3 copy-start
  195.2 31.4 %copy-start.3 = (f32[5120]{0:T(1024)S(1)}, f32[5120]{0:T(1024)}, u32[]{:S(2)}) copy-start(f32[5120]{0:T(1024)} %param.7) | copy-start | bytes 61444
  208.3 13.4 %all-to-all-start.5 = ((f32[16,1,20]{2,1,0:T(1,128)}), f32[16,1,20]{2,1,0:T(1,128)S(1)}, u32[]{:S(2)}, u32[]{:S(2)}) async-start(f32[16,1,20]{2,1,0:T(1,128)} %all_to_all.31), calls=%async_computation.6 | async-start | bytes 16384 | tf_op jit(solution)/shard_map/all_to_all | solution.py:65
  221.8 17.0 %all-to-all-start.3 = ((f32[16,20,512]{2,1,0:T(8,128)}), f32[16,20,512]{2,1,0:T(8,128)S(1)}, u32[]{:S(2)}, u32[]{:S(2)}) async-start(f32[16,20,512]{2,1,0:T(8,128)} %reshape.126), calls=%async_computation.4 | async-start | bytes 1572864 | tf_op jit(solution)/shard_map/all_to_all | solution.py:62
Sparse Core Ops, SparseCore 0:
  40.4 153.9 reduce-scatter.1
